TPU v7x, 256 devices: a whole 4x4x8 slice. The times are simulated.
256 devices in a mesh: tok: 32 (over z, x), head: 8 (over y, core).
Axes of the slice: x: 4, y: 4, z: 8, core: 2. Of those that a mesh axis runs over, the one named last changes fastest.
Arguments:
- embeddings: bfloat16 [4096, 4096], P('tok'), may hold values from -6 to 6
- norm_gain: bfloat16 [4096], replicated, may hold values from 0.099609375 to 1.8984375
- query_key_value_weight: bfloat16 [4096, 6144], P(None, 'head'), may hold values from -0.09375 to 0.09375
- embed_table: bfloat16 [65536, 4096], P('tok', 'head'), may hold values from -6 to 6
- rotated_cache_pages: bfloat16 [32, 32, 256, 2048], P('tok', None, None, 'head'), may hold values from -300 to 300
- page_owner_device: int32 [32, 32], P('tok'), may hold values from 0 to 31, each once within a row
- cached_length: int32 [32], P('tok'), may hold values from 2 to 8192, as said below
- vocab_shard: int32 [4096, 1], P('tok'), may hold values from 0 to 31; in each aligned block of 128 rows (0 to 127, 128 to 255, ...) at most 8 rows name the same one
- shard_row: int32 [4096], P('tok'), may hold values from 0 to 2047
- accept: int32 [4096], P('tok'), may hold values from 0 to 1, as said below
Outputs:
- out_first: bfloat16 [4096, 4096], P('tok', 'head')
- out_second: bfloat16 [4096, 4096], P('tok', 'head')
Inputs may be any that keep to these rules, and one draw needn't show every extreme that they name: `page_owner_device`: each row names every device of the tok axis once. `cached_length`: some request has exactly 8192 cached positions. `vocab_shard`: at most 8 of the 128 tokens of one request name the same shard, and some shard is named that often. `accept`: at most 32 accepted tokens in one request's block; some block has exactly 32.
All inputs are finite; a program needn't handle non-finite values.
Results may differ from a plain program's by a relative error of at most 0.017.
The roundings to bfloat16 on the way count: a program that leaves them out, or rounds other values in their place, can miss the bound.
Values may be sent and summed in bfloat16 or wider, within the bound.
No kernel may reach another device: no remote copies, remote signals or barrier semaphores. Data moves between devices by JAX's collectives and lax.ppermute only.
A program may use at most 128 MiB of HBM per device.

v0:
```python
import math
import jax
import jax.numpy as jnp
from jax import lax
from jax.sharding import PartitionSpec as P

QUERY_HEADS = 32
KEY_VALUE_HEADS = 8
HEAD_SIZE = 128
THETA = 500000.0


def angles(positions):
    steps_half = jnp.arange(HEAD_SIZE // 2, dtype=jnp.float32)
    frequency = THETA ** (-(steps_half * 2.0) / HEAD_SIZE)
    return positions.astype(jnp.float32)[:, None] * frequency[None, :]


def rotate(vectors, turning):
    half_width = vectors.shape[-1] // 2
    former = vectors[..., :half_width]
    latter = vectors[..., half_width:]
    cosine = jnp.cos(turning)
    sine_of = jnp.sin(turning)
    return jnp.concatenate(
        [former * cosine - latter * sine_of, latter * cosine + former * sine_of], axis=-1
    )


def project(inputs, norm_gain, query_key_value_weight, positions):
    widened = inputs.astype(jnp.float32)
    inverse = lax.rsqrt(jnp.mean(widened * widened, axis=-1, keepdims=True) + 1e-05)
    normed = (widened * inverse * norm_gain.astype(jnp.float32)).astype(jnp.bfloat16)
    combined = jnp.dot(normed, query_key_value_weight, preferred_element_type=jnp.float32)
    heads_per_group = QUERY_HEADS // KEY_VALUE_HEADS
    combined = combined.reshape(inputs.shape[0], -1, heads_per_group + 2, HEAD_SIZE)
    turning = angles(positions)[:, None, None, :]
    query_vectors = rotate(combined[:, :, :heads_per_group], turning).astype(jnp.bfloat16)
    block_keys = rotate(combined[:, :, heads_per_group : heads_per_group + 1], turning)[
        :, :, 0
    ].astype(jnp.bfloat16)
    block_values = combined[:, :, heads_per_group + 1].astype(jnp.bfloat16)
    return (query_vectors, block_keys, block_values)


def attend(query_vectors, block_keys, block_values, page_keys, page_values, usable):
    factor = 1.0 / math.sqrt(HEAD_SIZE)
    scores_cache = (
        jnp.einsum("bgqd,kgd->gqbk", query_vectors, page_keys, preferred_element_type=jnp.float32)
        * factor
    )
    scores_cache = jnp.where(usable[None, None, None, :], scores_cache, -1e30)
    scores_block = (
        jnp.einsum("bgqd,cgd->gqbc", query_vectors, block_keys, preferred_element_type=jnp.float32)
        * factor
    )
    highest = jnp.maximum(jnp.max(scores_cache, axis=-1), jnp.max(scores_block, axis=-1))[..., None]
    exp_cache = jnp.exp(scores_cache - highest)
    exp_block = jnp.exp(scores_block - highest)
    totals = jnp.sum(exp_cache, axis=-1) + jnp.sum(exp_block, axis=-1)
    weights_cache = exp_cache.astype(jnp.bfloat16)
    weights_block = exp_block.astype(jnp.bfloat16)
    combined = jnp.einsum(
        "gqbk,kgd->bgqd", weights_cache, page_values, preferred_element_type=jnp.float32
    )
    combined = combined + jnp.einsum(
        "gqbc,cgd->bgqd", weights_block, block_values, preferred_element_type=jnp.float32
    )
    result = combined / jnp.transpose(totals, (2, 0, 1))[..., None]
    return result.astype(jnp.bfloat16).reshape(query_vectors.shape[0], -1)


def body(
    embeddings,
    norm_gain,
    query_key_value_weight,
    embed_table,
    rotated_cache_pages,
    page_owner_device,
    cached_length,
    vocab_shard,
    shard_row,
    accept,
):
    members = lax.axis_size("tok")
    length = embeddings.shape[0]
    sources = jnp.arange(members, dtype=jnp.int32)
    positions = cached_length[0] + jnp.arange(length, dtype=jnp.int32)
    query_vectors, block_keys, block_values = project(
        embeddings, norm_gain, query_key_value_weight, positions
    )
    arrived = lax.all_to_all(rotated_cache_pages, "tok", split_axis=1, concat_axis=0, tiled=True)
    page_size = arrived.shape[2]
    arrived = arrived.reshape(members * page_size, -1, 2, HEAD_SIZE)
    page_index = jnp.sum(
        jnp.where(page_owner_device[0][:, None] == sources[None, :], sources[:, None], 0), axis=0
    )
    page_spots = page_index[:, None] * page_size + jnp.arange(page_size, dtype=jnp.int32)[None, :]
    usable = page_spots.reshape(-1) < cached_length[0]
    page_keys = arrived[:, :, 0]
    page_values = arrived[:, :, 1]

    def run_attention(query_rows, key_rows, value_rows):
        return attend(query_rows, key_rows, value_rows, page_keys, page_values, usable)

    output_one = run_attention(query_vectors, block_keys, block_values)
    target_shard = vocab_shard[:, 0]
    capacity = max(2, 2 * length // members)
    chosen = (target_shard[:, None] == sources[None, :]).astype(jnp.int32)
    earlier = (jnp.arange(length)[:, None] > jnp.arange(length)[None, :]).astype(jnp.int32)
    slot_rank = jnp.sum(jnp.dot(earlier, chosen) * chosen, axis=1)
    wanted = jnp.zeros((members, capacity), jnp.int32).at[target_shard, slot_rank].set(shard_row)
    found_rows = jnp.take(
        embed_table, lax.all_to_all(wanted, "tok", split_axis=0, concat_axis=0, tiled=True), axis=0
    )
    returned = lax.all_to_all(found_rows, "tok", split_axis=0, concat_axis=0, tiled=True)
    replacement = returned[target_shard, slot_rank]
    full_rows = lax.all_gather(replacement, "head", axis=1, tiled=True)
    replaced = jnp.where(accept[:, None] == 1, full_rows, embeddings)
    queries_two, keys_two, values_two = project(
        replaced, norm_gain, query_key_value_weight, positions
    )
    output_two = run_attention(queries_two, keys_two, values_two)
    return (output_one, output_two)


def solution(mesh):
    return jax.shard_map(
        body,
        mesh=mesh,
        in_specs=(
            P("tok", None),
            P(),
            P(None, "head"),
            P("tok", "head"),
            P("tok", None, None, "head"),
            P("tok", None),
            P("tok"),
            P("tok", None),
            P("tok"),
            P("tok"),
        ),
        out_specs=(P("tok", "head"), P("tok", "head")),
        check_vma=False,
    )
```

profile of v0, /device:TPU:12, one launch (start us, length us, event | category | flops | bytes accessed | tf_op | source)
XLA Modules:
  0.0 241.9 jit_solution(14365437352633551345)
XLA Ops:
  7.2 0.0 copy-start
  7.2 1.0 fusion.36
  8.2 0.7 fusion.89
  8.8 10.9 %scatter_fusion = s32[32,8]{0,1:T(8,128)S(1)} fusion(s32[32,8]{0,1:T(8,128)S(1)} %broadcast_in_dim.55, s32[128]{0:T(128)S(1)} %get-tuple-element.14, s32[128]{0:T(128)} %param.18), kind=kCustom, calls=%fused_computation.2 | custom fusion | bytes 2560 | tf_op jit(solution)/shard_map/scatter | solution.py:112
  19.8 0.1 copy.91
  19.9 19.1 %all_to_all.29 = s32[32,1,8]{2,1,0:T(1,128)S(1)} all-to-all(s32[32,1,8]{2,1,0:T(1,128)S(1)} %copy.91), channel_id=1, replica_groups=mesh['tok'=32,'head'=8] {'tok'}, dimensions={0} | all-to-all | bytes 2048 | tf_op jit(solution)/shard_map/all_to_all | solution.py:114
  38.9 0.1 reshape.410
  39.0 0.1 copy.92
  39.1 0.1 copy.93
  39.2 0.0 copy-start.6
  39.3 1.2 gather_fusion
  40.4 0.1 bitcast_select_fusion.2
  40.5 15.1 %all_to_all.30 = bf16[32,8,512]{2,1,0:T(8,128)(2,1)S(1)} all-to-all(bf16[32,8,512]{2,1,0:T(8,128)(2,1)S(1)} %bitcast_select_fusion.2), channel_id=1, replica_groups=mesh['tok'=32,'head'=8] {'tok'}, dimensions={0} | all-to-all | bytes 524288 | tf_op jit(solution)/shard_map/all_to_all | solution.py:116
  55.6 6.6 %all-to-all-start = ((bf16[1,32,256,256]{3,2,0,1:T(8,128)(2,1)}), bf16[1,32,256,256]{3,2,0,1:T(8,128)(2,1)}, u32[]{:S(2)}, u32[]{:S(2)}) async-start(bf16[1,32,256,256]{3,2,0,1:T(8,128)(2,1)} %bitcast.163), calls=%async_computation | async-start | bytes 8388608 | tf_op jit(solution)/shard_map/all_to_all | solution.py:92
  62.2 0.0 all-gather.2.cloned.1.call-start
  62.3 1.9 gather_fusion.1
  64.2 0.0 all-gather.2.cloned.1.call-update
  64.9 0.1 select_reduce_fusion
  65.0 0.1 add_compare_fusion
  65.2 0.3 multiply_cosine_fusion
  65.5 25.3 %all-gather.2.cloned.1.call-done = bf16[128,4096]{1,0:T(8,128)(2,1)} async-done(((bf16[128,512]{1,0:T(8,128)(2,1)}), bf16[128,4096]{1,0:T(8,128)(2,1)}) %all-gather.2.cloned.1.call-update) | async-done | bytes 1048592 | tf_op jit(solution)/shard_map/all_gather | solution.py:118
  90.8 1.9 fusion.17
  92.7 5.8 %fusion.41 = f32[128,768]{0,1:T(8,128)S(1)} fusion(bf16[4096,768]{1,0:T(8,128)(2,1)} %param.12, f32[128]{0:T(128)S(1)} %get-tuple-element.44, f32[4096]{0:T(1024)S(1)} %convert_element_type.83, bf16[128,4096]{1,0:T(8,128)(2,1)} %all-gather.2.cloned.1.call-done, bf16[128,4096]{1,0:T(8,128)(2,1)S(1)} %copy-done.3, pred[128]{0:T(512)(128)(4,1)S(1)} %broadcast_compare_fusion), kind=kOutput, calls=%fused_computation.48 | convolution fusion | flops 807927808 | bytes 8798848 | tf_op jit(solution)/shard_map/dot_general | solution.py:34
  98.6 0.1 copy.116
  98.7 0.1 copy.115
  98.8 5.4 %fusion.43 = f32[128,768]{0,1:T(8,128)S(1)} fusion(bf16[4096,768]{1,0:T(8,128)(2,1)} %param.12, bf16[128,4096]{1,0:T(8,128)(2,1)S(1)} %copy-done.3, f32[4096]{0:T(1024)S(1)} %convert_element_type.83, f32[128]{0:T(128)S(1)} %get-tuple-element.45), kind=kOutput, calls=%fused_computation.49 | convolution fusion | flops 807403520 | bytes 7750144 | tf_op jit(solution)/shard_map/dot_general | solution.py:34
  104.3 0.1 copy.111
  104.4 0.1 copy.112
  104.5 0.2 fusion.76
  104.8 0.1 fusion.59
  104.9 0.3 fusion.99
  105.2 0.3 fusion.101
  105.5 49.8 %all-to-all-done = bf16[1,32,256,256]{3,2,0,1:T(8,128)(2,1)} async-done(((bf16[1,32,256,256]{3,2,0,1:T(8,128)(2,1)}), bf16[1,32,256,256]{3,2,0,1:T(8,128)(2,1)}, u32[]{:S(2)}, u32[]{:S(2)}) %all-to-all-start) | async-done | bytes 4194336 | tf_op jit(solution)/shard_map/all_to_all | solution.py:92
  155.3 6.9 %reshape.435 = bf16[8192,1,2,128]{3,2,0,1:T(2,128)(2,1)} reshape(bf16[1,32,256,256]{3,2,0,1:T(8,128)(2,1)} %all-to-all-done) | data formatting | bytes 8388608 | tf_op jit(solution)/shard_map/reshape | solution.py:94
  162.3 9.8 %fusion.95 = (bf16[8192,1,1,128]{3,2,0,1:T(2,128)(2,1)S(1)}, bf16[8192,1,1,128]{3,2,0,1:T(2,128)(2,1)}) fusion(bf16[8192,1,2,128]{3,2,0,1:T(2,128)(2,1)} %reshape.435), kind=kLoop, calls=%fused_computation.135 | loop fusion | bytes 8388608 | tf_op jit(solution)/shard_map/slice | solution.py:100
  172.1 8.3 %fusion.98 = (f32[4,128]{1,0:T(4,128)}, f32[1,4,128,8192]{3,2,1,0:T(8,128)}) fusion(bf16[8192,1,1,128]{3,2,0,1:T(2,128)(2,1)S(1)} %get-tuple-element.16, bf16[128,4,64]{2,0,1:T(8,128)(2,1)S(1)} %get-tuple-element.30, bf16[128,4,64]{2,0,1:T(8,128)(2,1)S(1)} %get-tuple-element.31, pred[8192]{0:T(1024)(128)(4,1)S(1)} %lt.48), kind=kOutput, calls=%fused_computation.138 | convolution fusion | flops 1086586368 | bytes 19015680 | tf_op jit(solution)/shard_map/bgqd,kgd->gqbk/dot_general | solution.py:49
  180.3 7.7 %fusion.100 = (f32[4,128]{1,0:T(4,128)S(1)}, f32[1,4,128,8192]{3,2,1,0:T(8,128)}) fusion(bf16[8192,1,1,128]{3,2,0,1:T(2,128)(2,1)S(1)} %get-tuple-element.16, bf16[128,4,64]{2,0,1:T(8,128)(2,1)S(1)} %get-tuple-element.19, bf16[128,4,64]{2,0,1:T(8,128)(2,1)S(1)} %get-tuple-element.18, pred[8192]{0:T(1024)(128)(4,1)S(1)} %lt.48), kind=kOutput, calls=%fused_computation.140 | convolution fusion | flops 1086586368 | bytes 19015680 | tf_op jit(solution)/shard_map/bgqd,kgd->gqbk/dot_general | solution.py:49
  188.0 8.3 %copy.114 = bf16[8192,1,1,128]{0,3,2,1:T(8,128)(2,1)S(1)} copy(bf16[8192,1,1,128]{3,2,0,1:T(2,128)(2,1)} %get-tuple-element.17) | data formatting | bytes 4194304
  196.4 8.9 %fusion.2 = f32[4,128]{1,0:T(4,128)S(1)} fusion(f32[1,4,128,8192]{3,2,1,0:T(8,128)} %get-tuple-element.37, f32[4,128]{1,0:T(4,128)S(1)} %max.18), kind=kLoop, calls=%fused_computation.9 | loop fusion | flops 8388096 | bytes 16781312 | tf_op jit(solution)/shard_map/reduce_sum | solution.py:60
  205.2 8.8 %fusion.26 = f32[128,4,128]{2,0,1:T(8,128)S(1)} fusion(bf16[8192,1,1,128]{0,3,2,1:T(8,128)(2,1)S(1)} %copy.114, f32[1,4,128,8192]{3,2,1,0:T(8,128)} %get-tuple-element.37, f32[4,128]{1,0:T(4,128)S(1)} %max.18), kind=kOutput, calls=%fused_computation.40 | convolution fusion | flops 1082130432 | bytes 19138560 | tf_op jit(solution)/shard_map/gqbk,kgd->bgqd/dot_general | solution.py:63
  214.0 8.4 %fusion.31 = f32[128,4,128]{2,0,1:T(8,128)S(1)} fusion(bf16[8192,1,1,128]{0,3,2,1:T(8,128)(2,1)} %copy-done.2, f32[1,4,128,8192]{3,2,1,0:T(8,128)} %get-tuple-element.41, f32[4,128]{1,0:T(4,128)S(1)} %max.19), kind=kOutput, calls=%fused_computation.41 | convolution fusion | flops 1082130432 | bytes 19138560 | tf_op jit(solution)/shard_map/gqbk,kgd->bgqd/dot_general | solution.py:63
  222.4 8.1 %fusion.4 = f32[4,128]{1,0:T(4,128)S(1)} fusion(f32[1,4,128,8192]{3,2,1,0:T(8,128)} %get-tuple-element.41, f32[4,128]{1,0:T(4,128)S(1)} %max.19), kind=kLoop, calls=%fused_computation.11 | loop fusion | flops 8388096 | bytes 16781312 | tf_op jit(solution)/shard_map/reduce_sum | solution.py:60
  230.5 0.1 fusion.49
  230.6 0.9 fusion.38
  231.5 1.7 copy.99
  233.1 0.1 fusion.51
  233.2 1.0 fusion.40
  234.3 0.8 copy.100
  (33 shorter events, 0.2 us)
Async XLA Ops:
  7.2 32.0 %copy-start = (bf16[2048,512]{1,0:T(8,128)(2,1)S(1)}, bf16[2048,512]{1,0:T(8,128)(2,1)}, u32[]{:S(2)}) copy-start(bf16[2048,512]{1,0:T(8,128)(2,1)} %param.13) | copy-start | bytes 6291460
  39.2 25.1 %copy-start.6 = (bf16[4096]{0:T(1024)(128)(2,1)S(1)}, bf16[4096]{0:T(1024)(128)(2,1)}, u32[]{:S(2)}) copy-start(bf16[4096]{0:T(1024)(128)(2,1)} %param.11) | copy-start | bytes 24580
  39.2 25.7 %copy-start.7 = (s32[1,32]{1,0:T(1,128)S(1)}, s32[1,32]{1,0:T(1,128)}, u32[]{:S(2)}) copy-start(s32[1,32]{1,0:T(1,128)} %param.15) | copy-start | bytes 388
  39.2 25.9 %copy-start.8 = (s32[128]{0:T(128)S(1)}, s32[128]{0:T(128)}, u32[]{:S(2)}) copy-start(s32[128]{0:T(128)} %param.19) | copy-start | bytes 1540
  39.2 51.6 %copy-start.3 = (bf16[128,4096]{1,0:T(8,128)(2,1)S(1)}, bf16[128,4096]{1,0:T(8,128)(2,1)}, u32[]{:S(2)}) copy-start(bf16[128,4096]{1,0:T(8,128)(2,1)} %param.10) | copy-start | bytes 3145732
  55.6 99.7 %all-to-all-start = ((bf16[1,32,256,256]{3,2,0,1:T(8,128)(2,1)}), bf16[1,32,256,256]{3,2,0,1:T(8,128)(2,1)}, u32[]{:S(2)}, u32[]{:S(2)}) async-start(bf16[1,32,256,256]{3,2,0,1:T(8,128)(2,1)} %bitcast.163), calls=%async_computation | async-start | bytes 8388608 | tf_op jit(solution)/shard_map/all_to_all | solution.py:92
  62.2 28.6 %all-gather.2.cloned.1.call-start = ((), (), s32[]{:S(2)}) async-start(), calls=%async_computation.3 | async-start | bytes 1179648 | tf_op jit(solution)/shard_map/all_gather | solution.py:118
  98.5 6.7 %copy-start.4 = (f32[128,768]{0,1:T(8,128)}, f32[128,768]{0,1:T(8,128)S(1)}, u32[]{:S(2)}) copy-start(f32[128,768]{0,1:T(8,128)S(1)} %fusion.41) | copy-start | bytes 1179652
  188.0 8.4 %copy-start.5 = (f32[4,128]{1,0:T(4,128)S(1)}, f32[4,128]{1,0:T(4,128)}, u32[]{:S(2)}) copy-start(f32[4,128]{1,0:T(4,128)} %get-tuple-element.36) | copy-start | bytes 6148
  196.4 8.9 %copy-start.2 = (bf16[8192,1,1,128]{0,3,2,1:T(8,128)(2,1)}, bf16[8192,1,1,128]{0,3,2,1:T(8,128)(2,1)S(1)}, u32[]{:S(2)}) copy-start(bf16[8192,1,1,128]{0,3,2,1:T(8,128)(2,1)S(1)} %copy.114) | copy-start | bytes 6291460
  214.0 21.0 %copy-start.1 = (bf16[2048,512]{1,0:T(8,128)(2,1)S(1)}, bf16[2048,512]{1,0:T(8,128)(2,1)}, u32[]{:S(2)}) copy-start(bf16[2048,512]{1,0:T(8,128)(2,1)} %param.13) | copy-start | bytes 6291460
Sparse Core Ops, SparseCore 0:
  65.5 25.3 all-gather.1
where the time goes:
time: 243 us; the launch traced here: 242 us
  waiting for transfers between devices  75.2 us (31%)
  matrix products  47.7 us (20%)
  local copies, waits for them, and re-layouts  42.5 us (17%)
  blocking collectives  34.2 us (14%)
  other arithmetic  20.6 us (8%)
  between operations  15 us (6%)
  starting transfers between devices  6.66 us (3%)
    all_to_all x1, waiting for transfers between devices, body(): lax.all_to_all(rotated_cache_pages, 'tok', split_axis=1, concat_axis=0, t...  49.8 us
    all_gather x1, waiting for transfers between devices, body(): full_rows = lax.all_gather(replacement, 'head', axis=1, tiled=True)  25.3 us
    all_to_all x1, blocking collectives, body(): lax.all_to_all(wanted, 'tok', split_axis=0, concat_axis=0, tiled=True)  19.1 us
    dot_general x2, matrix products, attend(): jnp.einsum('gqbk,kgd->bgqd', weights_cache, page_values, preferred_elemen...  17.1 us
    reduce_sum x4, other arithmetic, attend(): totals = jnp.sum(exp_cache, axis=-1) + jnp.sum(exp_block, axis=-1)  17.1 us
    dot_general x2, matrix products, attend(): jnp.einsum('bgqd,kgd->gqbk', query_vectors, page_keys, preferred_element_...  15.9 us
    all_to_all x1, blocking collectives, body(): lax.all_to_all(found_rows, 'tok', split_axis=0, concat_axis=0, tiled=True)  15.1 us
    unnamed x25, local copies, waits for them, and re-layouts  11.3 us
  transfers between devices with their start and end apart: 2, of which 2 were waited for; matrix products, arithmetic and copies ran while one was open for 7% of the time, Pallas kernels for 0%

commit v1 on v0

--- a/solution.py
+++ b/solution.py
@@ -89,7 +89,12 @@
     query_vectors, block_keys, block_values = project(
         embeddings, norm_gain, query_key_value_weight, positions
     )
-    arrived = lax.all_to_all(rotated_cache_pages, "tok", split_axis=1, concat_axis=0, tiled=True)
+    arrived = jnp.concatenate(
+        lax.all_to_all(
+            jnp.stack(jnp.split(rotated_cache_pages, lax.axis_size("tok"), axis=1)), "tok", 0, 0
+        ),
+        axis=0,
+    )
     page_size = arrived.shape[2]
     arrived = arrived.reshape(members * page_size, -1, 2, HEAD_SIZE)
     page_index = jnp.sum(

time: 243 us -> 275 us (1.13)
  local copies, waits for them, and re-layouts: 42.5 us -> 92.1 us
  blocking collectives: 34.2 us -> 0 us
  starting transfers between devices: 6.66 us -> 27.8 us
  matrix products: 47.7 us -> 40.4 us
  waiting for transfers between devices: 75.2 us -> 80.6 us
  other arithmetic: 20.6 us -> 15.7 us
    unnamed x25 -> x58, local copies, waits for them, and re-layouts: 11.3 us -> 58.8 us
    all_to_all x2 -> x0, blocking collectives: 34.2 us -> none  [the longest x1 19.1 us: body(): lax.all_to_all(wanted, 'tok', split_axis=0, concat_axis=0, tiled=True)]
    all_to_all x1 -> x3, starting transfers between devices: 6.62 us -> 27.7 us  [the longest x1 11.6 us: body(): lax.all_to_all(wanted, 'tok', split_axis=0, concat_axis=0, tiled=True)]
    another operation x0 -> x2, local copies, waits for them, and re-layouts: none -> 8.5 us  [the longest x1 6.92 us: body(): arrived = arrived.reshape(members * page_size, -1, 2, HEAD_SIZE)]
    reshape x1 -> x0, local copies, waits for them, and re-layouts: 6.92 us -> none  [body(): arrived = arrived.reshape(members * page_size, -1, 2, HEAD_SIZE)]
    reduce_sum x4 -> x3, other arithmetic: 17.1 us -> 11.5 us  [attend(): totals = jnp.sum(exp_cache, axis=-1) + jnp.sum(exp_block, axis=-1)]
    dot_general x2, matrix products: 17.1 us -> 11.8 us  [attend(): jnp.einsum('gqbk,kgd->bgqd', weights_cache, page_values, preferred_elemen...]
    all_to_all x1 -> x3, waiting for transfers between devices: 49.8 us -> 55.2 us  [the longest x1 49.2 us: body(): lax.all_to_all(jnp.stack(jnp.split(rotated_cache_pages, lax.axis_size('to...]
  transfers between devices with their start and end apart: 2 -> 4, of which waited for: 2 -> 3; matrix products, arithmetic and copies ran while one was open for 7% -> 25% of each run, Pallas kernels for 0% -> 0%
where the time goes in v1:
time: 275 us; the launch traced here: 272 us
  local copies, waits for them, and re-layouts  92.1 us (33%)
  waiting for transfers between devices  80.6 us (29%)
  matrix products  40.4 us (15%)
  starting transfers between devices  27.8 us (10%)
  other arithmetic  15.7 us (6%)
  between operations  15 us (5%)
    unnamed x58, local copies, waits for them, and re-layouts  58.8 us
    all_to_all x1, waiting for transfers between devices, body(): lax.all_to_all(jnp.stack(jnp.split(rotated_cache_pages, lax.axis_size('to...  49.2 us
    all_gather x1, waiting for transfers between devices, body(): full_rows = lax.all_gather(replacement, 'head', axis=1, tiled=True)  25.4 us
    dot_general x2, matrix products, attend(): jnp.einsum('bgqd,kgd->gqbk', query_vectors, page_keys, preferred_element_...  14.7 us
    dot_general x2, matrix products, attend(): jnp.einsum('gqbk,kgd->bgqd', weights_cache, page_values, preferred_elemen...  11.8 us
    all_to_all x1, starting transfers between devices, body(): lax.all_to_all(wanted, 'tok', split_axis=0, concat_axis=0, tiled=True)  11.6 us
    reduce_sum x3, other arithmetic, attend(): totals = jnp.sum(exp_cache, axis=-1) + jnp.sum(exp_block, axis=-1)  11.5 us
    dot_general x2, matrix products, project(): jnp.dot(normed, query_key_value_weight, preferred_element_type=jnp.float32)  11.1 us
  transfers between devices with their start and end apart: 4, of which 3 were waited for; matrix products, arithmetic and copies ran while one was open for 25% of the time, Pallas kernels for 0%

profile of v1, /device:TPU:12, one launch (start us, length us, event | category | flops | bytes accessed | tf_op | source)
XLA Modules:
  0.0 271.6 jit_solution(3139468339772748646)
XLA Ops:
  8.8 10.9 %scatter_fusion = s32[32,8]{0,1:T(8,128)S(1)} fusion(s32[32,8]{0,1:T(8,128)S(1)} %broadcast_in_dim.55, s32[128]{0:T(128)S(1)} %get-tuple-element.18, s32[128]{0:T(128)} %param.18), kind=kCustom, calls=%fused_computation.2 | custom fusion | bytes 2560 | tf_op jit(solution)/shard_map/scatter | solution.py:117
  20.5 11.6 %all-to-all-start.1 = ((s32[32,1,8]{2,1,0:T(1,128)}), s32[32,1,8]{2,1,0:T(1,128)S(1)}, u32[]{:S(2)}, u32[]{:S(2)}) async-start(s32[32,1,8]{2,1,0:T(1,128)} %copy.97), calls=%async_computation.1 | async-start | bytes 32768 | tf_op jit(solution)/shard_map/all_to_all | solution.py:119
  32.1 1.6 bitcast_dynamic-update-slice_fusion.31
  35.2 1.6 bitcast_dynamic-update-slice_fusion.29
  36.7 1.6 bitcast_dynamic-update-slice_fusion.28
  38.3 1.6 bitcast_dynamic-update-slice_fusion.27
  39.9 1.6 bitcast_dynamic-update-slice_fusion.26
  41.4 1.6 bitcast_dynamic-update-slice_fusion.25
  43.0 1.6 bitcast_dynamic-update-slice_fusion.24
  46.1 1.6 bitcast_dynamic-update-slice_fusion.22
  47.7 1.6 bitcast_dynamic-update-slice_fusion.21
  49.2 1.6 bitcast_dynamic-update-slice_fusion.20
  50.8 1.6 bitcast_dynamic-update-slice_fusion.19
  52.4 1.6 bitcast_dynamic-update-slice_fusion.18
  53.9 1.6 bitcast_dynamic-update-slice_fusion.17
  55.5 1.6 bitcast_dynamic-update-slice_fusion.16
  57.1 1.6 bitcast_dynamic-update-slice_fusion.15
  58.6 1.6 bitcast_dynamic-update-slice_fusion.14
  60.2 1.6 bitcast_dynamic-update-slice_fusion.13
  61.8 1.6 bitcast_dynamic-update-slice_fusion.12
  63.3 1.6 bitcast_dynamic-update-slice_fusion.11
  64.9 1.6 bitcast_dynamic-update-slice_fusion.10
  66.4 1.6 bitcast_dynamic-update-slice_fusion.9
  68.0 1.6 bitcast_dynamic-update-slice_fusion.8
  69.6 1.6 bitcast_dynamic-update-slice_fusion.7
  71.1 1.6 bitcast_dynamic-update-slice_fusion.6
  72.7 1.6 bitcast_dynamic-update-slice_fusion.5
  74.2 1.6 bitcast_dynamic-update-slice_fusion.4
  79.6 9.8 %all-to-all-start.2 = ((bf16[32,8,512]{2,1,0:T(8,128)(2,1)}), bf16[32,8,512]{2,1,0:T(8,128)(2,1)S(1)}, u32[]{:S(2)}, u32[]{:S(2)}) async-start(bf16[32,8,512]{2,1,0:T(8,128)(2,1)} %bitcast_select_fusion.2), calls=%async_computation.2 | async-start | bytes 524288 | tf_op jit(solution)/shard_map/all_to_all | solution.py:121
  89.4 1.6 bitcast_dynamic-update-slice_fusion.2
  90.9 1.6 bitcast_dynamic-update-slice_fusion.1
  92.5 1.6 bitcast_dynamic-update-slice_fusion
  94.1 5.9 %all-to-all-done.2 = bf16[32,8,512]{2,1,0:T(8,128)(2,1)S(1)} async-done(((bf16[32,8,512]{2,1,0:T(8,128)(2,1)}), bf16[32,8,512]{2,1,0:T(8,128)(2,1)S(1)}, u32[]{:S(2)}, u32[]{:S(2)}) %all-to-all-start.2) | async-done | bytes 262176 | tf_op jit(solution)/shard_map/all_to_all | solution.py:121
  100.0 6.4 %all-to-all-start = ((bf16[32,1,1,256,256]{4,3,2,1,0:T(8,128)(2,1)}), bf16[32,1,1,256,256]{4,3,2,1,0:T(8,128)(2,1)}, u32[]{:S(2)}, u32[]{:S(2)}) async-start(bf16[32,1,1,256,256]{4,3,2,1,0:T(8,128)(2,1)} %bitcast_dynamic-update-slice_fusion), calls=%async_computation | async-start | bytes 8388608 | tf_op jit(solution)/shard_map/all_to_all | solution.py:93
  106.4 1.9 gather_fusion.1
  109.6 25.4 %all-gather.2.cloned.1.call-done = bf16[128,4096]{1,0:T(8,128)(2,1)} async-done(((bf16[128,512]{1,0:T(8,128)(2,1)}), bf16[128,4096]{1,0:T(8,128)(2,1)}) %all-gather.2.cloned.1.call-update) | async-done | bytes 1048592 | tf_op jit(solution)/shard_map/all_gather | solution.py:123
  135.0 1.9 fusion.17
  136.9 5.7 %fusion.31 = f32[128,768]{0,1:T(8,128)S(1)} fusion(bf16[4096,768]{1,0:T(8,128)(2,1)} %param.12, f32[128]{0:T(128)S(1)} %get-tuple-element.45, f32[4096]{0:T(1024)S(1)} %convert_element_type.83, bf16[128,4096]{1,0:T(8,128)(2,1)} %all-gather.2.cloned.1.call-done, bf16[128,4096]{1,0:T(8,128)(2,1)S(1)} %copy-done.3, pred[128]{0:T(512)(128)(4,1)S(1)} %broadcast_compare_fusion), kind=kOutput, calls=%fused_computation.48 | convolution fusion | flops 807927808 | bytes 8798848 | tf_op jit(solution)/shard_map/dot_general | solution.py:34
  143.0 5.4 %fusion.33 = f32[128,768]{0,1:T(8,128)S(1)} fusion(bf16[4096,768]{1,0:T(8,128)(2,1)} %param.12, bf16[128,4096]{1,0:T(8,128)(2,1)S(1)} %copy-done.3, f32[4096]{0:T(1024)S(1)} %convert_element_type.83, f32[128]{0:T(128)S(1)} %get-tuple-element.46), kind=kOutput, calls=%fused_computation.49 | convolution fusion | flops 807403520 | bytes 7750144 | tf_op jit(solution)/shard_map/dot_general | solution.py:34
  149.6 49.2 %all-to-all-done = bf16[32,1,1,256,256]{4,3,2,1,0:T(8,128)(2,1)} async-done(((bf16[32,1,1,256,256]{4,3,2,1,0:T(8,128)(2,1)}), bf16[32,1,1,256,256]{4,3,2,1,0:T(8,128)(2,1)}, u32[]{:S(2)}, u32[]{:S(2)}) %all-to-all-start) | async-done | bytes 4194336 | tf_op jit(solution)/shard_map/all_to_all | solution.py:93
  198.8 6.9 %reshape.423 = bf16[8192,1,2,128]{3,2,0,1:T(2,128)(2,1)} reshape(bf16[32,1,1,256,256]{4,3,2,1,0:T(8,128)(2,1)} %all-to-all-done) | data formatting | bytes 8388608 | tf_op jit(solution)/shard_map/reshape;reshape | solution.py:99
  205.7 9.8 %fusion.91 = (bf16[8192,1,1,128]{3,2,0,1:T(2,128)(2,1)}, bf16[8192,1,1,128]{3,2,0,1:T(2,128)(2,1)}) fusion(bf16[8192,1,2,128]{3,2,0,1:T(2,128)(2,1)} %reshape.423), kind=kLoop, calls=%fused_computation.173 | loop fusion | bytes 8388608 | tf_op jit(solution)/shard_map/slice | solution.py:106
  215.5 8.3 %copy.120 = bf16[8192,1,1,128]{0,3,2,1:T(8,128)(2,1)S(1)} copy(bf16[8192,1,1,128]{3,2,0,1:T(2,128)(2,1)} %get-tuple-element.20) | data formatting | bytes 4194304
  223.9 5.4 %fusion.40 = f32[8192,128,4]{1,0,2:T(8,128)S(1)} fusion(bf16[8192,1,1,128]{3,2,0,1:T(2,128)(2,1)} %get-tuple-element.21, bf16[128,4,64]{2,0,1:T(8,128)(2,1)S(1)} %get-tuple-element.34, bf16[128,4,64]{2,0,1:T(8,128)(2,1)S(1)} %get-tuple-element.35), kind=kOutput, calls=%fused_computation.56 | convolution fusion | flops 1074003968 | bytes 19005440 | tf_op jit(solution)/shard_map/bgqd,kgd->gqbk/dot_general | solution.py:49
  229.3 9.3 %bitcast_reduce_fusion = (f32[4,128]{1,0:T(4,128)S(1)}, f32[4,128]{1,0:T(4,128)S(1)}, f32[8192,128,4]{1,0,2:T(8,128)}) fusion(pred[8192]{0:T(1024)(128)(4,1)S(1)} %lt.48, f32[8192,128,4]{1,0,2:T(8,128)S(1)} %fusion.40, bf16[128,4,64]{2,0,1:T(8,128)(2,1)S(1)} %get-tuple-element.23, bf16[128,4,64]{2,0,1:T(8,128)(2,1)S(1)} %get-tuple-element.22, ...), kind=kOutput, calls=%fused_computation.4 | convolution fusion | flops 1099168768 | bytes 35794944 | tf_op jit(solution)/shard_map/bgqd,kgd->gqbk/dot_general | solution.py:49
  238.6 3.6 %fusion.8 = f32[128,4,128]{2,0,1:T(8,128)S(1)} fusion(f32[8192,128,4]{1,0,2:T(8,128)S(1)} %fusion.40, f32[4,128]{1,0:T(4,128)S(1)} %max.18, pred[8192]{0:T(1024)(128)(4,1)S(1)} %lt.48, bf16[8192,1,1,128]{0,3,2,1:T(8,128)(2,1)S(1)} %copy.120), kind=kOutput, calls=%fused_computation.17 | convolution fusion | flops 1090519040 | bytes 19146752 | tf_op jit(solution)/shard_map/gqbk,kgd->bgqd/dot_general | solution.py:63
  242.2 11.4 %fusion.4 = (f32[4,128]{1,0:T(4,128)S(1)}, f32[4,128]{1,0:T(4,128)S(1)}) fusion(f32[8192,128,4]{1,0,2:T(8,128)} %get-tuple-element.40, f32[4,128]{1,0:T(4,128)S(1)} %max.19, pred[8192]{0:T(1024)(128)(4,1)S(1)} %lt.48, f32[4,128]{1,0:T(4,128)S(1)} %max.18, f32[8192,128,4]{1,0,2:T(8,128)S(1)} %fusion.40), kind=kLoop, calls=%fused_computation.13 | loop fusion | flops 33553408 | bytes 33570816 | tf_op jit(solution)/shard_map/reduce_sum | solution.py:60
  253.6 8.2 %fusion.10 = f32[128,4,128]{2,0,1:T(8,128)S(1)} fusion(f32[8192,128,4]{1,0,2:T(8,128)} %get-tuple-element.40, f32[4,128]{1,0:T(4,128)S(1)} %max.19, pred[8192]{0:T(1024)(128)(4,1)S(1)} %lt.48, bf16[8192,1,1,128]{0,3,2,1:T(8,128)(2,1)S(1)} %copy-done.5), kind=kOutput, calls=%fused_computation.18 | convolution fusion | flops 1090519040 | bytes 19146752 | tf_op jit(solution)/shard_map/gqbk,kgd->bgqd/dot_general | solution.py:63
  (68 shorter events, 14.2 us)
Async XLA Ops:
  7.2 70.5 %copy-start = (bf16[2048,512]{1,0:T(8,128)(2,1)S(1)}, bf16[2048,512]{1,0:T(8,128)(2,1)}, u32[]{:S(2)}) copy-start(bf16[2048,512]{1,0:T(8,128)(2,1)} %param.13) | copy-start | bytes 6291460
  20.5 56.9 %all-to-all-start.1 = ((s32[32,1,8]{2,1,0:T(1,128)}), s32[32,1,8]{2,1,0:T(1,128)S(1)}, u32[]{:S(2)}, u32[]{:S(2)}) async-start(s32[32,1,8]{2,1,0:T(1,128)} %copy.97), calls=%async_computation.1 | async-start | bytes 32768 | tf_op jit(solution)/shard_map/all_to_all | solution.py:119
  79.6 20.4 %all-to-all-start.2 = ((bf16[32,8,512]{2,1,0:T(8,128)(2,1)}), bf16[32,8,512]{2,1,0:T(8,128)(2,1)S(1)}, u32[]{:S(2)}, u32[]{:S(2)}) async-start(bf16[32,8,512]{2,1,0:T(8,128)(2,1)} %bitcast_select_fusion.2), calls=%async_computation.2 | async-start | bytes 524288 | tf_op jit(solution)/shard_map/all_to_all | solution.py:121
  94.1 15.0 %copy-start.8 = (s32[1,32]{1,0:T(1,128)S(1)}, s32[1,32]{1,0:T(1,128)}, u32[]{:S(2)}) copy-start(s32[1,32]{1,0:T(1,128)} %param.15) | copy-start | bytes 388
  94.1 15.2 %copy-start.7 = (bf16[4096]{0:T(1024)(128)(2,1)S(1)}, bf16[4096]{0:T(1024)(128)(2,1)}, u32[]{:S(2)}) copy-start(bf16[4096]{0:T(1024)(128)(2,1)} %param.11) | copy-start | bytes 24580
  94.1 15.2 %copy-start.9 = (s32[128]{0:T(128)S(1)}, s32[128]{0:T(128)}, u32[]{:S(2)}) copy-start(s32[128]{0:T(128)} %param.19) | copy-start | bytes 1540
  94.1 41.0 %copy-start.3 = (bf16[128,4096]{1,0:T(8,128)(2,1)S(1)}, bf16[128,4096]{1,0:T(8,128)(2,1)}, u32[]{:S(2)}) copy-start(bf16[128,4096]{1,0:T(8,128)(2,1)} %param.10) | copy-start | bytes 3145732
  100.0 98.8 %all-to-all-start = ((bf16[32,1,1,256,256]{4,3,2,1,0:T(8,128)(2,1)}), bf16[32,1,1,256,256]{4,3,2,1,0:T(8,128)(2,1)}, u32[]{:S(2)}, u32[]{:S(2)}) async-start(bf16[32,1,1,256,256]{4,3,2,1,0:T(8,128)(2,1)} %bitcast_dynamic-update-slice_fusion), calls=%async_computation | async-start | bytes 8388608 | tf_op jit(solution)/shard_map/all_to_all | solution.py:93
  106.4 28.7 %all-gather.2.cloned.1.call-start = ((), (), s32[]{:S(2)}) async-start(), calls=%async_computation.3 | async-start | bytes 1179648 | tf_op jit(solution)/shard_map/all_gather | solution.py:123
  142.7 6.0 %copy-start.6 = (f32[128,768]{0,1:T(8,128)}, f32[128,768]{0,1:T(8,128)S(1)}, u32[]{:S(2)}) copy-start(f32[128,768]{0,1:T(8,128)S(1)} %fusion.31) | copy-start | bytes 1179652
  223.9 14.7 %copy-start.4 = (bf16[8192,1,1,128]{0,3,2,1:T(8,128)(2,1)}, bf16[8192,1,1,128]{0,3,2,1:T(8,128)(2,1)S(1)}, u32[]{:S(2)}) copy-start(bf16[8192,1,1,128]{0,3,2,1:T(8,128)(2,1)S(1)} %copy.120) | copy-start | bytes 6291460
  223.9 5.4 %copy-start.2 = (bf16[8192,1,1,128]{3,2,0,1:T(2,128)(2,1)S(1)}, bf16[8192,1,1,128]{3,2,0,1:T(2,128)(2,1)}, u32[]{:S(2)}) copy-start(bf16[8192,1,1,128]{3,2,0,1:T(2,128)(2,1)} %get-tuple-element.21) | copy-start | bytes 6291460
  242.2 11.4 %copy-start.5 = (bf16[8192,1,1,128]{0,3,2,1:T(8,128)(2,1)S(1)}, bf16[8192,1,1,128]{0,3,2,1:T(8,128)(2,1)}, u32[]{:S(2)}) copy-start(bf16[8192,1,1,128]{0,3,2,1:T(8,128)(2,1)} %copy-done.4) | copy-start | bytes 6291460
  253.6 11.2 %copy-start.1 = (bf16[2048,512]{1,0:T(8,128)(2,1)S(1)}, bf16[2048,512]{1,0:T(8,128)(2,1)}, u32[]{:S(2)}) copy-start(bf16[2048,512]{1,0:T(8,128)(2,1)} %param.13) | copy-start | bytes 6291460
Sparse Core Ops, SparseCore 0:
  109.6 25.3 all-gather.1
